TPU v7x, 32 devices: a whole 2x2x4 slice. The times are simulated.
32 devices in a mesh: rep: 2 (over y), seq: 4 (over z), head: 4 (over x, core).
Axes of the slice: x: 2, y: 2, z: 4, core: 2. Of those that a mesh axis runs over, the one named last changes fastest.
Arguments:
- queries: bfloat16 [3072, 2560], P(('rep', 'seq'), 'head'), parts along dimension 0, may hold values from -16 to 16
- keys: bfloat16 [3072, 2560], P(('rep', 'seq'), 'head'), parts along dimension 0, may hold values from -6 to 6
- values: bfloat16 [3072, 2560], P(('rep', 'seq'), 'head'), parts along dimension 0, may hold values from -6 to 6
- out_weight: bfloat16 [2560, 5120], P('seq', 'head'), may hold values from -0.3125 to 0.3125
- neighbours: int32 [8, 27], P('rep'), parts along dimension 0, may hold values from -1 to 3, as said below
- clip_ids: int32 [3072], P(('rep', 'seq')), parts along dimension 0, may hold values from 0 to 1
Outputs:
- output: bfloat16 [3072, 5120], P(('rep', 'seq'), 'head'), parts along dimension 0
There are 2 independent parts, one for each index of `rep`. A program takes and returns all parts, laid end to end along the dimension named above; an argument that names none is the same for every part. Nothing has to cross between parts.
Inputs may be any that keep to these rules, and one draw needn't show every extreme that they name: `neighbours`: column 9 (a + 1) + 3 (b + 1) + (c + 1) of row s, for a, b, c each -1, 0 or 1, is either -1 or s + a * 4 * 7 + b * 7 + c; column 13 of row s is s.
All inputs are finite; a program needn't handle non-finite values.
Results may differ from a plain program's by a relative error of at most 0.0058.
Values may be sent and summed in bfloat16 or wider, within the bound.
No kernel may reach another device: no remote copies, remote signals or barrier semaphores. Data moves between devices by JAX's collectives and lax.ppermute only.
A program may use at most 192 MiB of HBM per device.

v0:
```python
import math
import jax
import jax.numpy as jnp
from jax import lax
from jax.sharding import PartitionSpec as P

HD = 128
TGH = 4
TGW = 7


def from_behind(value, axis, by):
    peers = lax.axis_size(axis)
    pairs = [(i, i + by) for i in range(peers) if 0 <= i + by < peers]
    return lax.ppermute(value, axis, pairs)


def attend_head(query_head, key_head, value_head, allowed):
    scores = lax.dot_general(
        query_head, key_head, (((1,), (1,)), ((), ())), preferred_element_type=jnp.float32
    ) * (1.0 / math.sqrt(query_head.shape[1]))
    masked = jnp.where(allowed, scores, -1e30)
    highest = jnp.max(masked, axis=1, keepdims=True)
    raised = jnp.where(allowed, jnp.exp(masked - highest), 0.0)
    summed = jnp.sum(raised, axis=1, keepdims=True)
    weights = (raised / summed).astype(jnp.bfloat16)
    return jnp.dot(weights, value_head, preferred_element_type=jnp.float32).astype(jnp.bfloat16)


def on_device(queries, keys, values, out_weight, neighbours, clip_ids):
    tile_rows = queries.shape[0]
    feature_width = queries.shape[1]
    seq_count = lax.axis_size("seq")
    layer_tiles = TGH * TGW
    every_offset = set()
    for layer_step in (-1, 0, 1):
        for row_step in (-1, 0, 1):
            for col_step in (-1, 0, 1):
                every_offset.add(layer_step * layer_tiles + row_step * TGW + col_step)
    distances = [offset for offset in sorted(every_offset) if 0 < offset < seq_count]
    key_list = [keys]
    value_list = [values]
    clip_list = [clip_ids]
    offsets = [0]
    for distance in distances:
        below_keys, below_values, below_clips = from_behind(
            (keys, values, clip_ids), "seq", distance
        )
        above_keys, above_values, above_clips = from_behind(
            (keys, values, clip_ids), "seq", -distance
        )
        key_list += [below_keys, above_keys]
        value_list += [below_values, above_values]
        clip_list += [below_clips, above_clips]
        offsets += [distance, -distance]
    key_stack = jnp.stack(key_list)
    value_stack = jnp.stack(value_list)
    clip_stack = jnp.stack(clip_list)
    blocks = key_stack.shape[0]
    position = lax.axis_index("seq")
    window_row = lax.dynamic_index_in_dim(neighbours, position, 0, keepdims=False)
    sources = position - jnp.asarray(offsets, dtype=jnp.int32)
    present = jnp.any(
        (window_row[None, :] == sources[:, None]) & (window_row[None, :] >= 0), axis=1
    )
    key_clips = clip_stack.reshape(blocks * tile_rows)
    allowed = jnp.repeat(present, tile_rows)[None, :] & (clip_ids[:, None] == key_clips[None, :])
    key_rows = key_stack.reshape(blocks * tile_rows, feature_width)
    value_rows = value_stack.reshape(blocks * tile_rows, feature_width)
    head_outputs = []
    for head_index in range(feature_width // HD):
        first_col = head_index * HD
        head_outputs.append(
            attend_head(
                queries[:, first_col : first_col + HD],
                key_rows[:, first_col : first_col + HD],
                value_rows[:, first_col : first_col + HD],
                allowed,
            )
        )
    attended = jnp.concatenate(head_outputs, axis=1)
    all_features = lax.all_gather(attended, "head", axis=1, tiled=True)
    empty = jnp.zeros((tile_rows, out_weight.shape[1]), jnp.float32)
    weight_piece = lax.all_gather(out_weight, "seq", axis=0, tiled=True)
    features = lax.slice_in_dim(all_features, 0, weight_piece.shape[0], axis=1)
    projected = empty + jnp.dot(features, weight_piece, preferred_element_type=jnp.float32)
    return projected.astype(jnp.bfloat16)


def solution(mesh):
    in_specs = (
        P(("rep", "seq"), "head"),
        P(("rep", "seq"), "head"),
        P(("rep", "seq"), "head"),
        P("seq", "head"),
        P("rep", None),
        P(("rep", "seq")),
    )
    out_specs = P(("rep", "seq"), "head")
    return jax.shard_map(
        on_device, mesh=mesh, in_specs=in_specs, out_specs=out_specs, check_vma=False
    )
```

profile of v0, /device:TPU:0, one launch (start us, length us, event | category | flops | bytes accessed | tf_op | source)
XLA Modules:
  0.0 208.0 jit_solution(14518805611755408136)
XLA Ops:
  6.5 0.0 copy-start.2
  6.5 0.0 copy-start.3
  6.5 0.0 all-gather.3.cloned.1.call-start
  6.5 5.0 %collective-permute-start = (s32[384]{0:T(512)}, s32[384]{0:T(512)S(1)}, u32[]{:S(2)}, u32[]{:S(2)}) collective-permute-start(s32[384]{0:T(512)} %param.12), channel_id=1, source_target_pairs={{0,4},{4,8},{8,12},{1,5},{5,9},{9,13},{2,6},{6,10},{10,14},{3,7},{... | collective-permute-start | bytes 4616 | tf_op jit(solution)/shard_map/ppermute | solution.py:15
  11.6 1.3 collective-permute-start.1
  12.9 4.6 %collective-permute-start.2 = (bf16[384,640]{1,0:T(8,128)(2,1)}, bf16[384,640]{1,0:T(8,128)(2,1)S(1)}, u32[]{:S(2)}, u32[]{:S(2)}) collective-permute-start(bf16[384,640]{1,0:T(8,128)(2,1)} %param.8), channel_id=1, source_target_pairs={{0,4},{4,8},{8,12},{1,5},{5,9},{9,13},{2,6},{6,10},{10,14},{3,7},{... | collective-permute-start | bytes 1474568 | tf_op jit(solution)/shard_map/ppermute | solution.py:15
  17.5 1.3 collective-permute-start.3
  18.8 4.6 %collective-permute-start.4 = (bf16[384,640]{1,0:T(8,128)(2,1)}, bf16[384,640]{1,0:T(8,128)(2,1)S(1)}, u32[]{:S(2)}, u32[]{:S(2)}) collective-permute-start(bf16[384,640]{1,0:T(8,128)(2,1)} %param.9), channel_id=1, source_target_pairs={{0,4},{4,8},{8,12},{1,5},{5,9},{9,13},{2,6},{6,10},{10,14},{3,7},{... | collective-permute-start | bytes 1474568 | tf_op jit(solution)/shard_map/ppermute | solution.py:15
  23.4 0.7 compare_bitcast_fusion
  24.1 0.7 fusion.35
  24.8 0.7 broadcast_add_fusion
  25.4 0.2 and_reduce_fusion
  25.6 0.7 stack.36
  26.3 0.1 broadcast_in_dim.32
  26.4 0.0 collective-permute-done
  26.4 1.3 collective-permute-start.5
  27.7 0.0 collective-permute-done.1
  27.8 1.7 collective-permute-done.2
  29.4 4.3 %collective-permute-done.3 = bf16[384,640]{1,0:T(8,128)(2,1)S(1)} collective-permute-done((bf16[384,640]{1,0:T(8,128)(2,1)}, bf16[384,640]{1,0:T(8,128)(2,1)S(1)}, u32[]{:S(2)}, u32[]{:S(2)}) %collective-permute-start.3) | collective-permute-done | bytes 491552 | tf_op jit(solution)/shard_map/ppermute | solution.py:15
  33.8 1.2 pad_maximum_fusion
  35.0 0.0 copy-done.2
  35.0 0.0 copy-done.3
  35.0 0.6 fusion.41
  35.6 0.6 fusion.42
  36.3 0.6 fusion.43
  36.9 0.6 fusion.44
  37.5 0.0 copy-start
  37.5 0.6 fusion.45
  38.2 0.1 collective-permute-done.4
  38.2 4.0 %collective-permute-done.5 = bf16[384,640]{1,0:T(8,128)(2,1)S(1)} collective-permute-done((bf16[384,640]{1,0:T(8,128)(2,1)}, bf16[384,640]{1,0:T(8,128)(2,1)S(1)}, u32[]{:S(2)}, u32[]{:S(2)}) %collective-permute-start.5) | collective-permute-done | bytes 491552 | tf_op jit(solution)/shard_map/ppermute | solution.py:15
  42.2 0.0 copy-done
  42.3 0.2 pad_maximum_fusion.1
  42.4 2.3 %fusion.14 = (f32[384]{0:T(512)S(1)}, f32[384]{0:T(512)S(1)}, f32[384]{0:T(512)S(1)}, f32[384]{0:T(512)S(1)}, f32[384]{0:T(512)S(1)}) fusion(f32[384,1152]{0,1:T(8,128)S(1)} %get-tuple-element.11, f32[384]{0:T(512)S(1)} %get-tuple-element.10, s32[384]{0:T(512)S(1)} %copy-done.2, s32[1152]{0:T(1024)S(1)} %eq.35, pred[1152]{0:T(1024)(128)(4,1)S(1)} %and.24, ...), kind=kLoop, calls=%fused_computation.33 | loop fusion | flops 7518336 | bytes 8870016 | tf_op jit(solution)/shard_map/reduce_sum | solution.py:25
  44.7 1.0 fusion.15
  45.7 1.0 fusion.16
  46.8 1.0 fusion.17
  47.8 1.0 fusion.18
  48.8 1.0 fusion.19
  49.8 0.0 copy-start.1
  49.8 0.8 copy-done.1
  50.6 0.0 all-gather.3.cloned.1.call-update
  50.6 0.0 all-gather.5.cloned.1.call-start
  50.7 0.7 all-gather.5.cloned.1.call-update
  51.4 21.5 %all-gather.3.cloned.1.call-done = bf16[384,2560]{1,0:T(8,128)(2,1)} async-done(((bf16[384,640]{1,0:T(8,128)(2,1)}), bf16[384,2560]{1,0:T(8,128)(2,1)}) %all-gather.3.cloned.1.call-update) | async-done | bytes 1966096 | tf_op jit(solution)/shard_map/all_gather | solution.py:82
  72.8 121.2 %all-gather.5.cloned.1.call-done = bf16[2560,1280]{1,0:T(8,128)(2,1)} async-done(((bf16[640,1280]{1,0:T(8,128)(2,1)}), bf16[2560,1280]{1,0:T(8,128)(2,1)}) %all-gather.5.cloned.1.call-update) | async-done | bytes 6553616 | tf_op jit(solution)/shard_map/all_gather | solution.py:84
  194.1 7.1 %convolution_convert_fusion = bf16[384,1280]{1,0:T(8,128)(2,1)} fusion(bf16[384,2560]{1,0:T(8,128)(2,1)} %all-gather.3.cloned.1.call-done, bf16[2560,1280]{1,0:T(8,128)(2,1)} %all-gather.5.cloned.1.call-done), kind=kOutput, calls=%fused_computation.15 | convolution fusion | flops 2517073920 | bytes 9502720 | tf_op jit(solution)/shard_map/dot_general | solution.py:86
  (5 shorter events, 0.0 us)
Async XLA Ops:
  6.5 28.4 %copy-start.2 = (s32[384]{0:T(512)S(1)}, s32[384]{0:T(512)}, u32[]{:S(2)}) copy-start(s32[384]{0:T(512)} %param.12) | copy-start | bytes 4612
  6.5 28.5 %copy-start.3 = (bf16[384,640]{1,0:T(8,128)(2,1)S(1)}, bf16[384,640]{1,0:T(8,128)(2,1)}, u32[]{:S(2)}) copy-start(bf16[384,640]{1,0:T(8,128)(2,1)} %param.7) | copy-start | bytes 1474564
  6.5 66.3 %all-gather.3.cloned.1.call-start = ((), (), s32[]{:S(2)}) async-start(), calls=%async_computation | async-start | bytes 2457600 | tf_op jit(solution)/shard_map/all_gather | solution.py:82
  6.5 19.8 %collective-permute-start = (s32[384]{0:T(512)}, s32[384]{0:T(512)S(1)}, u32[]{:S(2)}, u32[]{:S(2)}) collective-permute-start(s32[384]{0:T(512)} %param.12), channel_id=1, source_target_pairs={{0,4},{4,8},{8,12},{1,5},{5,9},{9,13},{2,6},{6,10},{10,14},{3,7},{... | collective-permute-start | bytes 4616 | tf_op jit(solution)/shard_map/ppermute | solution.py:15
  11.6 16.1 %collective-permute-start.1 = (s32[384]{0:T(512)}, s32[384]{0:T(512)S(1)}, u32[]{:S(2)}, u32[]{:S(2)}) collective-permute-start(s32[384]{0:T(512)} %param.12), channel_id=1, source_target_pairs={{4,0},{8,4},{12,8},{5,1},{9,5},{13,9},{6,2},{10,6},{14,10},{7,3},{... | collective-permute-start | bytes 4616 | tf_op jit(solution)/shard_map/ppermute | solution.py:15
  12.9 16.5 %collective-permute-start.2 = (bf16[384,640]{1,0:T(8,128)(2,1)}, bf16[384,640]{1,0:T(8,128)(2,1)S(1)}, u32[]{:S(2)}, u32[]{:S(2)}) collective-permute-start(bf16[384,640]{1,0:T(8,128)(2,1)} %param.8), channel_id=1, source_target_pairs={{0,4},{4,8},{8,12},{1,5},{5,9},{9,13},{2,6},{6,10},{10,14},{3,7},{... | collective-permute-start | bytes 1474568 | tf_op jit(solution)/shard_map/ppermute | solution.py:15
  17.5 16.3 %collective-permute-start.3 = (bf16[384,640]{1,0:T(8,128)(2,1)}, bf16[384,640]{1,0:T(8,128)(2,1)S(1)}, u32[]{:S(2)}, u32[]{:S(2)}) collective-permute-start(bf16[384,640]{1,0:T(8,128)(2,1)} %param.8), channel_id=1, source_target_pairs={{4,0},{8,4},{12,8},{5,1},{9,5},{13,9},{6,2},{10,6},{14,10},{7,3},{... | collective-permute-start | bytes 1474568 | tf_op jit(solution)/shard_map/ppermute | solution.py:15
  18.8 19.4 %collective-permute-start.4 = (bf16[384,640]{1,0:T(8,128)(2,1)}, bf16[384,640]{1,0:T(8,128)(2,1)S(1)}, u32[]{:S(2)}, u32[]{:S(2)}) collective-permute-start(bf16[384,640]{1,0:T(8,128)(2,1)} %param.9), channel_id=1, source_target_pairs={{0,4},{4,8},{8,12},{1,5},{5,9},{9,13},{2,6},{6,10},{10,14},{3,7},{... | collective-permute-start | bytes 1474568 | tf_op jit(solution)/shard_map/ppermute | solution.py:15
  26.4 15.9 %collective-permute-start.5 = (bf16[384,640]{1,0:T(8,128)(2,1)}, bf16[384,640]{1,0:T(8,128)(2,1)S(1)}, u32[]{:S(2)}, u32[]{:S(2)}) collective-permute-start(bf16[384,640]{1,0:T(8,128)(2,1)} %param.9), channel_id=1, source_target_pairs={{4,0},{8,4},{12,8},{5,1},{9,5},{13,9},{6,2},{10,6},{14,10},{7,3},{... | collective-permute-start | bytes 1474568 | tf_op jit(solution)/shard_map/ppermute | solution.py:15
  37.5 4.7 %copy-start = (bf16[384,640]{1,0:T(8,128)(2,1)S(1)}, bf16[384,640]{1,0:T(8,128)(2,1)}, u32[]{:S(2)}) copy-start(bf16[384,640]{1,0:T(8,128)(2,1)} %param.9) | copy-start | bytes 1474564
  49.8 0.8 copy-start.1
  50.6 143.4 %all-gather.5.cloned.1.call-start = ((), (), s32[]{:S(2)}) async-start(), calls=%async_computation.1 | async-start | bytes 8192000 | tf_op jit(solution)/shard_map/all_gather | solution.py:84
Sparse Core Ops, SparseCore 0:
  50.7 22.0 all-gather.2
  74.4 119.6 all-gather.4
where the time goes:
time: 208 us
  waiting for transfers between devices  154 us (74%)
  starting transfers between devices  18.1 us (9%)
  matrix products  15.3 us (7%)
  between operations  13.6 us (7%)
  other arithmetic  5.25 us (3%)
  local copies, waits for them, and re-layouts  2.27 us (1%)
    all_gather x1, waiting for transfers between devices, on_device(): weight_piece = lax.all_gather(out_weight, 'seq', axis=0, tiled=True)  121 us
    all_gather x1, waiting for transfers between devices, on_device(): all_features = lax.all_gather(attended, 'head', axis=1, tiled=True)  21.5 us
    ppermute x6, starting transfers between devices, from_behind(): return lax.ppermute(value, axis, pairs)  18.1 us
    ppermute x6, waiting for transfers between devices, from_behind(): return lax.ppermute(value, axis, pairs)  10.1 us
    dot_general x1, matrix products, on_device(): jnp.dot(features, weight_piece, preferred_element_type=jnp.float32)  7.1 us
    dot_general x5, matrix products, attend_head(): jnp.dot(weights, value_head, preferred_element_type=jnp.float32)  5.04 us
  transfers between devices with their start and end apart: 8, of which 6 were waited for; matrix products, arithmetic and copies ran while one was open for 4% of the time, Pallas kernels for 0%

commit v1 on v0

--- a/solution.py
+++ b/solution.py
@@ -7,6 +7,23 @@
 HD = 128
 TGH = 4
 TGW = 7
+
+
+def track_the_shapes(original, where_dim):
+    axis_name = "head"
+    moved = lax.axis_size(axis_name)
+    later = lax.axis_index(axis_name)
+    even, d_next = (moved, later)
+    opened, tall = (original, 1)
+    while tall < even:
+        view_out = lax.ppermute(
+            opened, axis_name=axis_name, perm=list(map(lambda m: (m, m ^ tall), range(even)))
+        )
+        outer = jnp.concatenate([opened, view_out], where_dim)
+        shaped = jnp.concatenate([view_out, opened], where_dim)
+        opened = jnp.where(d_next & tall == 0, outer, shaped)
+        tall = 2 * tall
+    return opened
 
 
 def from_behind(value, axis, by):
@@ -79,7 +96,7 @@
             )
         )
     attended = jnp.concatenate(head_outputs, axis=1)
-    all_features = lax.all_gather(attended, "head", axis=1, tiled=True)
+    all_features = track_the_shapes(attended, 1)
     empty = jnp.zeros((tile_rows, out_weight.shape[1]), jnp.float32)
     weight_piece = lax.all_gather(out_weight, "seq", axis=0, tiled=True)
     features = lax.slice_in_dim(all_features, 0, weight_piece.shape[0], axis=1)

time: 208 us -> 159 us (0.76)
  waiting for transfers between devices: 154 us -> 104 us
    all_gather x1, waiting for transfers between devices: 121 us -> 39.1 us  [on_device(): weight_piece = lax.all_gather(out_weight, 'seq', axis=0, tiled=True)]
    ppermute x6, waiting for transfers between devices: 10.1 us -> 39.6 us  [from_behind(): return lax.ppermute(value, axis, pairs)]
    ppermute x0 -> x2, waiting for transfers between devices: none -> 24.1 us  [track_the_shapes(): lax.ppermute(opened, axis_name=axis_name, perm=list(map(lambda m: (m, m ^...]
    all_gather x1 -> x0, waiting for transfers between devices: 21.5 us -> none  [on_device(): all_features = lax.all_gather(attended, 'head', axis=1, tiled=True)]
  transfers between devices with their start and end apart: 8 -> 9, of which waited for: 6 -> 5; matrix products, arithmetic and copies ran while one was open for 4% -> 9% of each run, Pallas kernels for 0% -> 0%
where the time goes in v1:
time: 159 us; the launch traced here: 158 us
  waiting for transfers between devices  104 us (65%)
  starting transfers between devices  19.7 us (12%)
  matrix products  14.4 us (9%)
  between operations  13.6 us (9%)
  other arithmetic  4.34 us (3%)
  local copies, waits for them, and re-layouts  2.5 us (2%)
    ppermute x6, waiting for transfers between devices, from_behind(): return lax.ppermute(value, axis, pairs)  39.6 us
    all_gather x1, waiting for transfers between devices, on_device(): weight_piece = lax.all_gather(out_weight, 'seq', axis=0, tiled=True)  39.1 us
    ppermute x2, waiting for transfers between devices, track_the_shapes(): lax.ppermute(opened, axis_name=axis_name, perm=list(map(lambda m: (m, m ^...  24.1 us
    ppermute x6, starting transfers between devices, from_behind(): return lax.ppermute(value, axis, pairs)  18.1 us
    dot_general x1, matrix products, on_device(): jnp.dot(features, weight_piece, preferred_element_type=jnp.float32)  6.62 us
    dot_general x5, matrix products, attend_head(): jnp.dot(weights, value_head, preferred_element_type=jnp.float32)  4.64 us
  transfers between devices with their start and end apart: 9, of which 5 were waited for; matrix products, arithmetic and copies ran while one was open for 9% of the time, Pallas kernels for 0%

profile of v1, /device:TPU:0, one launch (start us, length us, event | category | flops | bytes accessed | tf_op | source)
XLA Modules:
  0.0 158.2 jit_solution(14815643945886860622)
XLA Ops:
  6.5 0.0 copy-start
  6.5 0.0 all-gather.2.cloned.1.call-start
  6.5 0.7 all-gather.2.cloned.1.call-update
  7.3 0.0 copy-start.1
  7.3 5.1 %collective-permute-start.2 = (bf16[384,640]{1,0:T(8,128)(2,1)}, bf16[384,640]{1,0:T(8,128)(2,1)S(1)}, u32[]{:S(2)}, u32[]{:S(2)}) collective-permute-start(bf16[384,640]{1,0:T(8,128)(2,1)} %param.8), channel_id=1, source_target_pairs={{0,4},{4,8},{8,12},{1,5},{5,9},{9,13},{2,6},{6,10},{10,14},{3,7},{... | collective-permute-start | bytes 1474568 | tf_op jit(solution)/shard_map/ppermute | solution.py:32
  12.4 1.3 collective-permute-start.3
  13.7 4.6 %collective-permute-start.4 = (bf16[384,640]{1,0:T(8,128)(2,1)}, bf16[384,640]{1,0:T(8,128)(2,1)S(1)}, u32[]{:S(2)}, u32[]{:S(2)}) collective-permute-start(bf16[384,640]{1,0:T(8,128)(2,1)} %param.9), channel_id=1, source_target_pairs={{0,4},{4,8},{8,12},{1,5},{5,9},{9,13},{2,6},{6,10},{10,14},{3,7},{... | collective-permute-start | bytes 1474568 | tf_op jit(solution)/shard_map/ppermute | solution.py:32
  18.2 1.3 collective-permute-start.5
  19.5 4.5 %collective-permute-start = (s32[384]{0:T(512)}, s32[384]{0:T(512)S(1)}, u32[]{:S(2)}, u32[]{:S(2)}) collective-permute-start(s32[384]{0:T(512)} %param.12), channel_id=1, source_target_pairs={{0,4},{4,8},{8,12},{1,5},{5,9},{9,13},{2,6},{6,10},{10,14},{3,7},{... | collective-permute-start | bytes 4616 | tf_op jit(solution)/shard_map/ppermute | solution.py:32
  24.1 0.7 broadcast_add_fusion
  24.8 0.7 compare_bitcast_fusion
  25.5 0.7 fusion.36
  26.1 21.0 %collective-permute-done = s32[384]{0:T(512)S(1)} collective-permute-done((s32[384]{0:T(512)}, s32[384]{0:T(512)S(1)}, u32[]{:S(2)}, u32[]{:S(2)}) %collective-permute-start) | collective-permute-done | bytes 1568 | tf_op jit(solution)/shard_map/ppermute | solution.py:32
  47.1 1.3 collective-permute-start.1
  48.4 0.2 and_reduce_fusion
  48.6 0.7 stack.36
  49.3 0.1 broadcast_in_dim.32
  49.4 18.6 %collective-permute-done.1 = s32[384]{0:T(512)S(1)} collective-permute-done((s32[384]{0:T(512)}, s32[384]{0:T(512)S(1)}, u32[]{:S(2)}, u32[]{:S(2)}) %collective-permute-start.1) | collective-permute-done | bytes 1568 | tf_op jit(solution)/shard_map/ppermute | solution.py:32
  68.0 0.0 collective-permute-done.2
  68.0 0.0 collective-permute-done.3
  68.0 0.0 copy-done
  68.0 0.2 pad_maximum_fusion
  68.2 0.0 copy-start.2
  68.3 0.0 copy-start.3
  68.3 0.0 collective-permute-done.4
  68.3 0.0 collective-permute-done.5
  68.3 0.0 copy-done.1
  68.3 0.2 pad_maximum_fusion.1
  68.5 0.4 copy-done.2
  68.9 0.4 copy-done.3
  69.3 0.6 fusion.43
  69.9 0.6 fusion.44
  70.6 0.6 fusion.45
  71.2 0.6 fusion.46
  71.8 0.6 fusion.47
  72.5 2.3 %fusion.20 = (f32[384]{0:T(512)S(1)}, f32[384]{0:T(512)S(1)}, f32[384]{0:T(512)S(1)}, f32[384]{0:T(512)S(1)}, f32[384]{0:T(512)S(1)}) fusion(f32[384,1152]{0,1:T(8,128)S(1)} %get-tuple-element.23, f32[384]{0:T(512)S(1)} %get-tuple-element.22, s32[384]{0:T(512)S(1)} %copy-done.2, s32[1152]{0:T(1024)S(1)} %eq.43, pred[1152]{0:T(1024)(128)(4,1)S(1)} %and.33, ...), kind=kLoop, calls=%fused_computation.40 | loop fusion | flops 7518336 | bytes 8870016 | tf_op jit(solution)/shard_map/reduce_sum | solution.py:42
  74.8 0.9 constant_dynamic-update-slice_fusion.4
  75.7 0.9 constant_dynamic-update-slice_fusion.3
  76.6 0.9 constant_dynamic-update-slice_fusion.2
  77.6 0.9 constant_dynamic-update-slice_fusion.1
  78.5 0.9 constant_dynamic-update-slice_fusion
  79.4 0.1 collective-permute-start.6
  79.5 1.8 %collective-permute-done.6 = bf16[384,640]{0,1:T(8,128)(2,1)S(1)} collective-permute-done((bf16[384,640]{0,1:T(8,128)(2,1)S(1)}, bf16[384,640]{0,1:T(8,128)(2,1)S(1)}, u32[]{:S(2)}, u32[]{:S(2)}) %collective-permute-start.6) | collective-permute-done | bytes 491552 | tf_op jit(solution)/shard_map/ppermute | solution.py:19
  81.4 0.1 constant_dynamic-update-slice_fusion.16
  81.6 0.1 broadcast_select_fusion
  81.7 1.6 collective-permute-start.7
  83.3 22.3 %collective-permute-done.7 = bf16[384,1280]{0,1:T(8,128)(2,1)S(1)} collective-permute-done((bf16[384,1280]{0,1:T(8,128)(2,1)S(1)}, bf16[384,1280]{0,1:T(8,128)(2,1)S(1)}, u32[]{:S(2)}, u32[]{:S(2)}) %collective-permute-start.7) | collective-permute-done | bytes 983072 | tf_op jit(solution)/shard_map/ppermute | solution.py:19
  105.6 39.1 %all-gather.2.cloned.1.call-done = bf16[2560,1280]{1,0:T(8,128)(2,1)} async-done(((bf16[640,1280]{1,0:T(8,128)(2,1)}), bf16[2560,1280]{1,0:T(8,128)(2,1)}) %all-gather.2.cloned.1.call-update) | async-done | bytes 6553616 | tf_op jit(solution)/shard_map/all_gather | solution.py:101
  144.7 6.6 %convolution_convert_fusion = bf16[384,1280]{1,0:T(8,128)(2,1)} fusion(bf16[2560,1280]{1,0:T(8,128)(2,1)} %all-gather.2.cloned.1.call-done, bf16[384,1280]{0,1:T(8,128)(2,1)S(1)} %collective-permute-done.7, bf16[384,1280]{0,1:T(8,128)(2,1)S(1)} %broadcast_select_fusion, pred[]{:T(512)S(6)} %eq.36), kind=kOutput, calls=%fused_computation.15 | convolution fusion | flops 2525921280 | bytes 9502721 | tf_op jit(solution)/shard_map/dot_general | solution.py:103
  (10 shorter events, 0.1 us)
Async XLA Ops:
  6.5 61.5 %copy-start = (bf16[384,640]{1,0:T(8,128)(2,1)S(1)}, bf16[384,640]{1,0:T(8,128)(2,1)}, u32[]{:S(2)}) copy-start(bf16[384,640]{1,0:T(8,128)(2,1)} %param.8) | copy-start | bytes 1474564
  6.5 138.2 %all-gather.2.cloned.1.call-start = ((), (), s32[]{:S(2)}) async-start(), calls=%async_computation | async-start | bytes 8192000 | tf_op jit(solution)/shard_map/all_gather | solution.py:101
  7.3 61.0 %copy-start.1 = (bf16[384,640]{1,0:T(8,128)(2,1)S(1)}, bf16[384,640]{1,0:T(8,128)(2,1)}, u32[]{:S(2)}) copy-start(bf16[384,640]{1,0:T(8,128)(2,1)} %param.9) | copy-start | bytes 1474564
  7.3 60.8 %collective-permute-start.2 = (bf16[384,640]{1,0:T(8,128)(2,1)}, bf16[384,640]{1,0:T(8,128)(2,1)S(1)}, u32[]{:S(2)}, u32[]{:S(2)}) collective-permute-start(bf16[384,640]{1,0:T(8,128)(2,1)} %param.8), channel_id=1, source_target_pairs={{0,4},{4,8},{8,12},{1,5},{5,9},{9,13},{2,6},{6,10},{10,14},{3,7},{... | collective-permute-start | bytes 1474568 | tf_op jit(solution)/shard_map/ppermute | solution.py:32
  12.4 55.7 %collective-permute-start.3 = (bf16[384,640]{1,0:T(8,128)(2,1)}, bf16[384,640]{1,0:T(8,128)(2,1)S(1)}, u32[]{:S(2)}, u32[]{:S(2)}) collective-permute-start(bf16[384,640]{1,0:T(8,128)(2,1)} %param.8), channel_id=1, source_target_pairs={{4,0},{8,4},{12,8},{5,1},{9,5},{13,9},{6,2},{10,6},{14,10},{7,3},{... | collective-permute-start | bytes 1474568 | tf_op jit(solution)/shard_map/ppermute | solution.py:32
  13.7 54.6 %collective-permute-start.4 = (bf16[384,640]{1,0:T(8,128)(2,1)}, bf16[384,640]{1,0:T(8,128)(2,1)S(1)}, u32[]{:S(2)}, u32[]{:S(2)}) collective-permute-start(bf16[384,640]{1,0:T(8,128)(2,1)} %param.9), channel_id=1, source_target_pairs={{0,4},{4,8},{8,12},{1,5},{5,9},{9,13},{2,6},{6,10},{10,14},{3,7},{... | collective-permute-start | bytes 1474568 | tf_op jit(solution)/shard_map/ppermute | solution.py:32
  18.2 50.0 %collective-permute-start.5 = (bf16[384,640]{1,0:T(8,128)(2,1)}, bf16[384,640]{1,0:T(8,128)(2,1)S(1)}, u32[]{:S(2)}, u32[]{:S(2)}) collective-permute-start(bf16[384,640]{1,0:T(8,128)(2,1)} %param.9), channel_id=1, source_target_pairs={{4,0},{8,4},{12,8},{5,1},{9,5},{13,9},{6,2},{10,6},{14,10},{7,3},{... | collective-permute-start | bytes 1474568 | tf_op jit(solution)/shard_map/ppermute | solution.py:32
  19.5 27.6 %collective-permute-start = (s32[384]{0:T(512)}, s32[384]{0:T(512)S(1)}, u32[]{:S(2)}, u32[]{:S(2)}) collective-permute-start(s32[384]{0:T(512)} %param.12), channel_id=1, source_target_pairs={{0,4},{4,8},{8,12},{1,5},{5,9},{9,13},{2,6},{6,10},{10,14},{3,7},{... | collective-permute-start | bytes 4616 | tf_op jit(solution)/shard_map/ppermute | solution.py:32
  47.1 20.9 %collective-permute-start.1 = (s32[384]{0:T(512)}, s32[384]{0:T(512)S(1)}, u32[]{:S(2)}, u32[]{:S(2)}) collective-permute-start(s32[384]{0:T(512)} %param.12), channel_id=1, source_target_pairs={{4,0},{8,4},{12,8},{5,1},{9,5},{13,9},{6,2},{10,6},{14,10},{7,3},{... | collective-permute-start | bytes 4616 | tf_op jit(solution)/shard_map/ppermute | solution.py:32
  68.2 0.7 copy-start.2
  68.3 1.0 copy-start.3
  79.4 1.9 %collective-permute-start.6 = (bf16[384,640]{0,1:T(8,128)(2,1)S(1)}, bf16[384,640]{0,1:T(8,128)(2,1)S(1)}, u32[]{:S(2)}, u32[]{:S(2)}) collective-permute-start(bf16[384,640]{0,1:T(8,128)(2,1)S(1)} %get-tuple-element.12), channel_id=1, source_target_pairs={{0,1},{1,0},{2,3},{3,2},{4,5},{5,4},{6,7},{7,6},{8,9},{9,8},{10,11... | collective-permute-start | bytes 1474568 | tf_op jit(solution)/shard_map/ppermute | solution.py:19
  81.7 23.9 %collective-permute-start.7 = (bf16[384,1280]{0,1:T(8,128)(2,1)S(1)}, bf16[384,1280]{0,1:T(8,128)(2,1)S(1)}, u32[]{:S(2)}, u32[]{:S(2)}) collective-permute-start(bf16[384,1280]{0,1:T(8,128)(2,1)S(1)} %broadcast_select_fusion), channel_id=1, source_target_pairs={{0,2},{1,3},{2,0},{3,1},{4,6},{5,7},{6,4},{7,5},{8,10},{9,11},{10,... | collective-permute-start | bytes 2949128 | tf_op jit(solution)/shard_map/ppermute | solution.py:19
Sparse Core Ops, SparseCore 0:
  8.9 135.7 all-gather.1
